TPU v7x, 256 devices: a whole 4x4x8 slice. The times are simulated.
256 devices in a mesh: aa: 32 (over z, x), ba: 8 (over y, core).
Axes of the slice: x: 4, y: 4, z: 8, core: 2. Of those that a mesh axis runs over, the one named last changes fastest.
Arguments:
- snapshots: float32 [8192, 65536], P(('aa', 'ba')), may hold values from -125 to 125
Outputs:
- factors: float32 [8, 64, 64], replicated
- pod_modes: float32 [8, 64, 65536], P(None, None, ('aa', 'ba'))
All inputs are finite; a program needn't handle non-finite values.
Results may differ from a plain program's by a relative error of at most 0.000098.
Values sent between devices are 32-bit elements; how exact they have to be, the bound alone decides.
No kernel may reach another device: no remote copies, remote signals or barrier semaphores. Data moves between devices by JAX's collectives and lax.ppermute only.
A program may use at most 128 MiB of HBM per device.

v0:
```python
import math
import jax
import jax.numpy as jnp
from jax import lax
from jax.sharding import PartitionSpec as P

FREQS = 8


def spectral_rows(block_len, points, first, count):
    sample = first + jnp.arange(count, dtype=jnp.int32)
    harmonic = jnp.arange(1, FREQS + 1, dtype=jnp.int32)
    phase_turns = (sample[:, None] * harmonic[None, :] % block_len).astype(jnp.float32) * (
        2.0 * math.pi / block_len
    )
    full = jnp.arange(block_len, dtype=jnp.int32).astype(jnp.float32) * (2.0 * math.pi / block_len)
    full_window = 0.5 - 0.5 * jnp.cos(full)
    norm_scale = 1.0 / jnp.sqrt(points * jnp.sum(full_window * full_window))
    sample_angle = sample.astype(jnp.float32) * (2.0 * math.pi / block_len)
    window = 0.5 - 0.5 * jnp.cos(sample_angle)
    cosine = window[:, None] * jnp.cos(phase_turns) * norm_scale
    sine = -window[:, None] * jnp.sin(phase_turns) * norm_scale
    return jnp.stack([cosine, sine], axis=1)


def local(snapshots):
    time_dev, points = snapshots.shape
    n_aa = lax.axis_size("aa")
    n_ba = lax.axis_size("ba")
    pts_dev = points // (n_aa * n_ba)
    block_len = time_dev * n_ba
    u = lax.axis_index("ba")
    table = spectral_rows(block_len, points, u * time_dev, time_dev)
    arranged = snapshots.reshape(time_dev, n_aa, n_ba, pts_dev)
    partial = jnp.einsum("savq,sgf->vgfaq", arranged, table, precision=lax.Precision.HIGHEST)
    block_spec = lax.psum_scatter(partial, "ba", scatter_dimension=0, tiled=True)
    spectra = lax.all_to_all(block_spec, "aa", split_axis=3, concat_axis=0, tiled=True)
    blocks = spectra.shape[0]
    columns = 2 * blocks
    cols = jnp.transpose(spectra.reshape(blocks, 2, FREQS, pts_dev), (2, 0, 1, 3)).reshape(
        FREQS, columns, pts_dev
    )
    product = jnp.einsum("fip,fjp->fij", cols, cols, precision=lax.Precision.HIGHEST)
    gram_sum = lax.psum(product, ("aa", "ba"))
    lower_factor = jnp.linalg.cholesky(gram_sum)
    identity = jnp.broadcast_to(jnp.eye(columns, dtype=gram_sum.dtype), lower_factor.shape)
    inverse = lax.linalg.triangular_solve(lower_factor, identity, left_side=True, lower=True)
    pod_modes = math.sqrt(points) * jnp.einsum(
        "fij,fjp->fip", inverse, cols, precision=lax.Precision.HIGHEST
    )
    return (jnp.swapaxes(lower_factor, 1, 2), pod_modes)


def solution(mesh):
    placed = (P(("aa", "ba"), None),)
    return jax.shard_map(
        local,
        mesh=mesh,
        in_specs=placed,
        out_specs=(P(), P(None, None, ("aa", "ba"))),
        check_vma=False,
    )
```

profile of v0, /device:TPU:2, one launch (start us, length us, event | category | flops | bytes accessed | tf_op | source)
XLA Modules:
  0.0 479.1 jit_solution(12910174082356562652)
XLA Ops:
  7.2 0.0 all-reduce.6.cloned.1.call-start
  7.3 0.6 multiply_reduce_fusion
  8.6 5.9 %copy.38 = f32[4,8,256,256]{3,2,1,0:T(8,128)S(1)} copy(f32[4,8,256,256]{3,1,2,0:T(8,128)} %bitcast.42) | data formatting | bytes 16777216
  14.6 0.1 multiply_multiply_fusion.1
  14.7 0.0 copy-start
  14.7 9.2 %fusion.3 = f32[8,2,8,32,256]{4,2,0,3,1:T(8,128)} fusion(f32[32,32,8,256]{3,2,1,0:T(8,128)S(1)} %bitcast.41, f32[32,1,8]{0,2,1:T(8,128)S(1)} %get-tuple-element.13, f32[32,1,8]{0,2,1:T(8,128)S(1)} %get-tuple-element.12), kind=kOutput, calls=%fused_computation.3 | convolution fusion | flops 402653696 | bytes 12584960 | tf_op jit(solution)/shard_map/savq,sgf->vgfaq/dot_general | solution.py:35
  23.9 0.0 all-reduce.6.cloned.1.call-update
  23.9 0.0 copy-done
  23.9 0.6 dynamic-slice
  24.5 80.1 %all-reduce.6.cloned.1.call-done = f32[8,2,8,32,256]{4,2,0,3,1:T(8,128)} async-done(((f32[8,2,8,32,256]{4,2,0,3,1:T(8,128)}), f32[8,2,8,32,256]{4,2,0,3,1:T(8,128)}) %all-reduce.6.cloned.1.call-update) | async-done | bytes 4194320
  104.6 1.7 constant_dynamic-slice_fusion
  106.3 0.9 copy.25
  107.2 10.1 %all-to-all-start = ((f32[1,2,8,32,256]{4,2,0,1,3:T(8,128)}), f32[1,2,8,32,256]{4,2,0,1,3:T(8,128)S(1)}, u32[]{:S(2)}, u32[]{:S(2)}) async-start(f32[1,2,8,32,256]{4,2,0,1,3:T(8,128)} %copy.25), calls=%async_computation | async-start | bytes 1048576 | tf_op jit(solution)/shard_map/all_to_all | solution.py:37
  117.3 0.2 all-reduce.4.cloned.1.call-start
  117.6 14.8 %all-to-all-done = f32[1,2,8,32,256]{4,2,0,1,3:T(8,128)S(1)} async-done(((f32[1,2,8,32,256]{4,2,0,1,3:T(8,128)}), f32[1,2,8,32,256]{4,2,0,1,3:T(8,128)S(1)}, u32[]{:S(2)}, u32[]{:S(2)}) %all-to-all-start) | async-done | bytes 524320 | tf_op jit(solution)/shard_map/all_to_all | solution.py:37
  132.4 1.6 fusion.7
  134.0 0.0 all-reduce.4.cloned.1.call-update
  134.0 246.7 %all-reduce.4.cloned.1.call-done = f32[8,64,64]{1,2,0:T(8,128)} async-done(((f32[8,64,64]{1,2,0:T(8,128)}), f32[8,64,64]{1,2,0:T(8,128)}) %all-reduce.4.cloned.1.call-update) | async-done | bytes 131088 | tf_op jit(solution)/shard_map/psum | solution.py:44
  380.7 1.1 copy.29
  381.8 1.0 fusion.11
  382.8 46.9 %custom-call.7 = f32[8,64,64]{2,1,0:T(8,128)S(1)} custom-call(f32[8,64,64]{2,1,0:T(8,128)S(1)} %fusion.11), custom_call_target="Cholesky" | custom-call | tf_op jit(solution)/shard_map/jit(cholesky)/cholesky | solution.py:45
  429.8 0.1 compare_reduce_fusion
  429.9 0.1 select_bitcast_fusion
  430.0 39.3 %custom-call.8 = f32[8,1,64,64]{2,3,1,0:T(8,128)S(1)} custom-call(f32[8,1,64,64]{3,2,1,0:T(8,128)S(1)} %get-tuple-element.10), custom_call_target="InvertDiagBlocksLowerTriangular" | custom-call | tf_op jit(solution)/shard_map/triangular_solve | solution.py:47
  469.3 0.6 fusion.9
  469.9 1.5 convolution_multiply_fusion
  471.5 0.8 copy.32
  (7 shorter events, 0.1 us)
Async XLA Ops:
  7.2 97.5 %all-reduce.6.cloned.1.call-start = ((), (), s32[]{:S(2)}) async-start(), calls=%async_computation.2 | async-start | bytes 8388608
  14.7 9.2 %copy-start = (u32[256]{0:T(256)S(1)}, u32[256]{0:T(256)}, u32[]{:S(2)}) copy-start(u32[256]{0:T(256)} %constant.81) | copy-start | bytes 3076
  107.2 25.2 %all-to-all-start = ((f32[1,2,8,32,256]{4,2,0,1,3:T(8,128)}), f32[1,2,8,32,256]{4,2,0,1,3:T(8,128)S(1)}, u32[]{:S(2)}, u32[]{:S(2)}) async-start(f32[1,2,8,32,256]{4,2,0,1,3:T(8,128)} %copy.25), calls=%async_computation | async-start | bytes 1048576 | tf_op jit(solution)/shard_map/all_to_all | solution.py:37
  117.3 263.4 %all-reduce.4.cloned.1.call-start = ((), (), s32[]{:S(2)}) async-start(), calls=%async_computation.1 | async-start | bytes 524288 | tf_op jit(solution)/shard_map/psum | solution.py:44
Sparse Core Ops, SparseCore 0:
  24.0 80.5 all-reduce.5
  134.1 246.5 all-reduce.3
where the time goes:
time: 479 us
  waiting for transfers between devices  342 us (71%)
  other arithmetic  88.3 us (18%)
  between operations  14.8 us (3%)
  matrix products  12.9 us (3%)
  local copies, waits for them, and re-layouts  11 us (2%)
  starting transfers between devices  10.4 us (2%)
    psum x1, waiting for transfers between devices, local(): gram_sum = lax.psum(product, ('aa', 'ba'))  247 us
    unnamed x3, waiting for transfers between devices  80.2 us
    another operation x4, other arithmetic, local(): lower_factor = jnp.linalg.cholesky(gram_sum)  47.1 us
    another operation x2, other arithmetic, local(): lax.linalg.triangular_solve(lower_factor, identity, left_side=True, lower...  39.4 us
    all_to_all x1, waiting for transfers between devices, local(): lax.all_to_all(block_spec, 'aa', split_axis=3, concat_axis=0, tiled=True)  14.8 us
    all_to_all x1, starting transfers between devices, local(): lax.all_to_all(block_spec, 'aa', split_axis=3, concat_axis=0, tiled=True)  10.1 us
  transfers between devices with their start and end apart: 3, of which 3 were waited for; matrix products, arithmetic and copies ran while one was open for 0% of the time, Pallas kernels for 0%

commit v1 on v0

--- a/solution.py
+++ b/solution.py
@@ -5,6 +5,14 @@
 from jax.sharding import PartitionSpec as P
 
 FREQS = 8
+
+
+def note_values(frame):
+    device_axis = "aa"
+    peer_axis = "ba"
+    for q in (peer_axis, device_axis):
+        frame = lax.psum(frame, q)
+    return frame
 
 
 def spectral_rows(block_len, points, first, count):
@@ -41,7 +49,7 @@
         FREQS, columns, pts_dev
     )
     product = jnp.einsum("fip,fjp->fij", cols, cols, precision=lax.Precision.HIGHEST)
-    gram_sum = lax.psum(product, ("aa", "ba"))
+    gram_sum = note_values(product)
     lower_factor = jnp.linalg.cholesky(gram_sum)
     identity = jnp.broadcast_to(jnp.eye(columns, dtype=gram_sum.dtype), lower_factor.shape)
     inverse = lax.linalg.triangular_solve(lower_factor, identity, left_side=True, lower=True)

time: 479 us -> 440 us (0.919)
  waiting for transfers between devices: 342 us -> 287 us
  blocking collectives: 0 us -> 25 us
  starting transfers between devices: 10.4 us -> 0.3 us
    psum x1 -> x2, waiting for transfers between devices: 247 us -> 207 us  [note_values(): frame = lax.psum(frame, q)]
    all_to_all x0 -> x1, blocking collectives: none -> 25 us  [local(): lax.all_to_all(block_spec, 'aa', split_axis=3, concat_axis=0, tiled=True)]
    all_to_all x1 -> x0, waiting for transfers between devices: 14.8 us -> none  [local(): lax.all_to_all(block_spec, 'aa', split_axis=3, concat_axis=0, tiled=True)]
    all_to_all x1 -> x0, starting transfers between devices: 10.1 us -> none  [local(): lax.all_to_all(block_spec, 'aa', split_axis=3, concat_axis=0, tiled=True)]
    unnamed x3 -> x4, waiting for transfers between devices: 80.2 us -> 80.1 us
where the time goes in v1:
time: 440 us; the launch traced here: 439 us
  waiting for transfers between devices  287 us (65%)
  other arithmetic  88.3 us (20%)
  blocking collectives  25 us (6%)
  between operations  14.5 us (3%)
  matrix products  12.9 us (3%)
  local copies, waits for them, and re-layouts  10.2 us (2%)
    psum x2, waiting for transfers between devices, note_values(): frame = lax.psum(frame, q)  207 us
    unnamed x4, waiting for transfers between devices  80.1 us
    another operation x4, other arithmetic, local(): lower_factor = jnp.linalg.cholesky(gram_sum)  47.1 us
    another operation x2, other arithmetic, local(): lax.linalg.triangular_solve(lower_factor, identity, left_side=True, lower...  39.4 us
    all_to_all x1, blocking collectives, local(): lax.all_to_all(block_spec, 'aa', split_axis=3, concat_axis=0, tiled=True)  25 us
    dot_general x1, matrix products, local(): jnp.einsum('savq,sgf->vgfaq', arranged, table, precision=lax.Precision.HI...  9.16 us
    unnamed x6, local copies, waits for them, and re-layouts  9.1 us
  transfers between devices with their start and end apart: 3, of which 3 were waited for; matrix products, arithmetic and copies ran while one was open for 0% of the time, Pallas kernels for 0%

profile of v1, /device:TPU:2, one launch (start us, length us, event | category | flops | bytes accessed | tf_op | source)
XLA Modules:
  0.0 438.5 jit_solution(10516754383478878791)
XLA Ops:
  7.2 0.0 all-reduce.9.cloned.1.call-start
  7.3 0.6 multiply_reduce_fusion
  8.6 5.9 %copy.38 = f32[4,8,256,256]{3,2,1,0:T(8,128)S(1)} copy(f32[4,8,256,256]{3,1,2,0:T(8,128)} %bitcast.42) | data formatting | bytes 16777216
  14.6 0.1 multiply_multiply_fusion.1
  14.7 0.0 copy-start
  14.7 9.2 %fusion.3 = f32[8,2,8,32,256]{4,2,0,3,1:T(8,128)} fusion(f32[32,32,8,256]{3,2,1,0:T(8,128)S(1)} %bitcast.41, f32[32,1,8]{0,2,1:T(8,128)S(1)} %get-tuple-element.13, f32[32,1,8]{0,2,1:T(8,128)S(1)} %get-tuple-element.12), kind=kOutput, calls=%fused_computation.3 | convolution fusion | flops 402653696 | bytes 12584960 | tf_op jit(solution)/shard_map/savq,sgf->vgfaq/dot_general | solution.py:43
  23.9 0.0 all-reduce.9.cloned.1.call-update
  23.9 0.0 all-reduce.5.cloned.1.call-start
  23.9 0.0 copy-done
  24.0 0.6 dynamic-slice
  24.5 80.1 %all-reduce.9.cloned.1.call-done = f32[8,2,8,32,256]{4,2,0,3,1:T(8,128)} async-done(((f32[8,2,8,32,256]{4,2,0,3,1:T(8,128)}), f32[8,2,8,32,256]{4,2,0,3,1:T(8,128)}) %all-reduce.9.cloned.1.call-update) | async-done | bytes 4194320
  104.6 1.7 constant_dynamic-slice_fusion
  106.3 0.1 copy.25
  106.4 25.0 %all_to_all.15 = f32[1,2,8,32,256]{4,2,0,1,3:T(8,128)S(1)} all-to-all(f32[1,2,8,32,256]{4,2,0,1,3:T(8,128)S(1)} %copy.25), channel_id=1, replica_groups=mesh['aa'=32,'ba'=8] {'aa'}, dimensions={3} | all-to-all | bytes 1048576 | tf_op jit(solution)/shard_map/all_to_all | solution.py:45
  131.4 1.6 fusion.7
  133.0 0.0 all-reduce.5.cloned.1.call-update
  133.0 0.2 all-reduce.7.cloned.1.call-start
  133.3 61.3 %all-reduce.5.cloned.1.call-done = f32[8,64,64]{1,2,0:T(8,128)} async-done(((f32[8,64,64]{1,2,0:T(8,128)}), f32[8,64,64]{1,2,0:T(8,128)}) %all-reduce.5.cloned.1.call-update) | async-done | bytes 131088 | tf_op jit(solution)/shard_map/psum | solution.py:14
  194.5 0.0 all-reduce.7.cloned.1.call-update
  194.6 145.8 %all-reduce.7.cloned.1.call-done = f32[8,64,64]{1,2,0:T(8,128)} async-done(((f32[8,64,64]{1,2,0:T(8,128)}), f32[8,64,64]{1,2,0:T(8,128)}) %all-reduce.7.cloned.1.call-update) | async-done | bytes 131088 | tf_op jit(solution)/shard_map/psum | solution.py:14
  340.4 1.1 copy.29
  341.5 1.0 fusion.11
  342.5 46.9 %custom-call.7 = f32[8,64,64]{2,1,0:T(8,128)S(1)} custom-call(f32[8,64,64]{2,1,0:T(8,128)S(1)} %fusion.11), custom_call_target="Cholesky" | custom-call | tf_op jit(solution)/shard_map/jit(cholesky)/cholesky | solution.py:53
  389.5 0.1 compare_reduce_fusion
  389.6 0.1 select_bitcast_fusion
  389.7 39.3 %custom-call.8 = f32[8,1,64,64]{2,3,1,0:T(8,128)S(1)} custom-call(f32[8,1,64,64]{3,2,1,0:T(8,128)S(1)} %get-tuple-element.10), custom_call_target="InvertDiagBlocksLowerTriangular" | custom-call | tf_op jit(solution)/shard_map/triangular_solve | solution.py:55
  429.0 0.6 fusion.9
  429.6 1.5 convolution_multiply_fusion
  431.1 0.8 copy.32
  (7 shorter events, 0.1 us)
Async XLA Ops:
  7.2 97.5 %all-reduce.9.cloned.1.call-start = ((), (), s32[]{:S(2)}) async-start(), calls=%async_computation.3 | async-start | bytes 8388608
  14.7 9.3 %copy-start = (u32[256]{0:T(256)S(1)}, u32[256]{0:T(256)}, u32[]{:S(2)}) copy-start(u32[256]{0:T(256)} %constant.81) | copy-start | bytes 3076
  23.9 170.6 %all-reduce.5.cloned.1.call-start = ((), (), s32[]{:S(2)}) async-start(), calls=%async_computation.1 | async-start | bytes 524288 | tf_op jit(solution)/shard_map/psum | solution.py:14
  133.0 207.4 %all-reduce.7.cloned.1.call-start = ((), (), s32[]{:S(2)}) async-start(), calls=%async_computation.2 | async-start | bytes 524288 | tf_op jit(solution)/shard_map/psum | solution.py:14
Sparse Core Ops, SparseCore 0:
  24.0 80.5 all-reduce.8
  133.1 61.3 all-reduce.4
  198.4 142.0 all-reduce.6

commit v2 on v0

--- a/solution.py
+++ b/solution.py
@@ -34,7 +34,12 @@
     arranged = snapshots.reshape(time_dev, n_aa, n_ba, pts_dev)
     partial = jnp.einsum("savq,sgf->vgfaq", arranged, table, precision=lax.Precision.HIGHEST)
     block_spec = lax.psum_scatter(partial, "ba", scatter_dimension=0, tiled=True)
-    spectra = lax.all_to_all(block_spec, "aa", split_axis=3, concat_axis=0, tiled=True)
+    spectra = jnp.concatenate(
+        lax.all_to_all(
+            jnp.stack(jnp.split(block_spec, lax.axis_size("aa"), 3), axis=0), "aa", 0, 0
+        ),
+        0,
+    )
     blocks = spectra.shape[0]
     columns = 2 * blocks
     cols = jnp.transpose(spectra.reshape(blocks, 2, FREQS, pts_dev), (2, 0, 1, 3)).reshape(

time: 479 us -> 542 us (1.13)
  local copies, waits for them, and re-layouts: 11 us -> 72.1 us
    unnamed x6 -> x36, local copies, waits for them, and re-layouts: 9.1 us -> 69.1 us
where the time goes in v2:
time: 542 us; the launch traced here: 540 us
  waiting for transfers between devices  341 us (63%)
  other arithmetic  88.3 us (16%)
  local copies, waits for them, and re-layouts  72.1 us (13%)
  between operations  14.8 us (3%)
  matrix products  12.9 us (2%)
  starting transfers between devices  10.4 us (2%)
    psum x1, waiting for transfers between devices, local(): gram_sum = lax.psum(product, ('aa', 'ba'))  247 us
    unnamed x3, waiting for transfers between devices  79.5 us
    unnamed x36, local copies, waits for them, and re-layouts  69.1 us
    another operation x4, other arithmetic, local(): lower_factor = jnp.linalg.cholesky(gram_sum)  47.1 us
    another operation x2, other arithmetic, local(): lax.linalg.triangular_solve(lower_factor, identity, left_side=True, lower...  39.4 us
    all_to_all x1, waiting for transfers between devices, local(): lax.all_to_all(jnp.stack(jnp.split(block_spec, lax.axis_size('aa'), 3), a...  14.8 us
  transfers between devices with their start and end apart: 3, of which 3 were waited for; matrix products, arithmetic and copies ran while one was open for 0% of the time, Pallas kernels for 0%

profile of v2, /device:TPU:2, one launch (start us, length us, event | category | flops | bytes accessed | tf_op | source)
XLA Modules:
  0.0 539.6 jit_solution(11308106750119786190)
XLA Ops:
  8.6 5.9 %copy.151 = f32[4,8,256,256]{3,2,1,0:T(8,128)S(1)} copy(f32[4,8,256,256]{3,1,2,0:T(8,128)} %bitcast.228) | data formatting | bytes 16777216
  14.7 9.2 %fusion.3 = f32[8,2,8,32,256]{4,2,0,3,1:T(8,128)} fusion(f32[32,32,8,256]{3,2,1,0:T(8,128)S(1)} %bitcast.227, f32[32,1,8]{0,2,1:T(8,128)S(1)} %get-tuple-element.11, f32[32,1,8]{0,2,1:T(8,128)S(1)} %get-tuple-element.10), kind=kOutput, calls=%fused_computation.3 | convolution fusion | flops 402653696 | bytes 12584960 | tf_op jit(solution)/shard_map/savq,sgf->vgfaq/dot_general | solution.py:35
  25.1 79.5 %all-reduce.6.cloned.1.call-done = f32[8,2,8,32,256]{4,2,0,3,1:T(8,128)} async-done(((f32[8,2,8,32,256]{4,2,0,3,1:T(8,128)}), f32[8,2,8,32,256]{4,2,0,3,1:T(8,128)}) %all-reduce.6.cloned.1.call-update) | async-done | bytes 4194320
  106.6 2.0 constant_dynamic-update-slice_fusion.30
  108.6 2.0 constant_dynamic-update-slice_fusion.29
  110.5 2.0 constant_dynamic-update-slice_fusion.28
  112.5 2.0 constant_dynamic-update-slice_fusion.27
  114.5 2.0 constant_dynamic-update-slice_fusion.26
  116.4 2.0 constant_dynamic-update-slice_fusion.25
  118.4 2.0 constant_dynamic-update-slice_fusion.24
  120.4 2.0 constant_dynamic-update-slice_fusion.23
  122.3 2.0 constant_dynamic-update-slice_fusion.22
  124.3 2.0 constant_dynamic-update-slice_fusion.21
  126.3 2.0 constant_dynamic-update-slice_fusion.20
  128.3 2.0 constant_dynamic-update-slice_fusion.19
  130.2 2.0 constant_dynamic-update-slice_fusion.18
  132.2 2.0 constant_dynamic-update-slice_fusion.17
  134.2 2.0 constant_dynamic-update-slice_fusion.16
  136.1 2.0 constant_dynamic-update-slice_fusion.15
  138.1 2.0 constant_dynamic-update-slice_fusion.14
  140.1 2.0 constant_dynamic-update-slice_fusion.13
  142.1 2.0 constant_dynamic-update-slice_fusion.12
  144.0 2.0 constant_dynamic-update-slice_fusion.11
  146.0 2.0 constant_dynamic-update-slice_fusion.10
  148.0 2.0 constant_dynamic-update-slice_fusion.9
  149.9 2.0 constant_dynamic-update-slice_fusion.8
  161.8 2.0 constant_dynamic-update-slice_fusion.2
  167.7 10.1 %all-to-all-start = ((f32[32,1,2,8,1,256]{5,3,2,4,1,0:T(8,128)}), f32[32,1,2,8,1,256]{5,3,2,4,1,0:T(8,128)S(1)}, u32[]{:S(2)}, u32[]{:S(2)}) async-start(f32[32,1,2,8,1,256]{5,3,2,4,1,0:T(8,128)} %constant_dynamic-update-slice_fusion), calls=%async_computation | async-start | bytes 1048576 | tf_op jit(solution)/shard_map/all_to_all | solution.py:38
  178.1 14.8 %all-to-all-done = f32[32,1,2,8,1,256]{5,3,2,4,1,0:T(8,128)S(1)} async-done(((f32[32,1,2,8,1,256]{5,3,2,4,1,0:T(8,128)}), f32[32,1,2,8,1,256]{5,3,2,4,1,0:T(8,128)S(1)}, u32[]{:S(2)}, u32[]{:S(2)}) %all-to-all-start) | async-done | bytes 524320 | tf_op jit(solution)/shard_map/all_to_all | solution.py:38
  194.5 246.7 %all-reduce.4.cloned.1.call-done = f32[8,64,64]{1,2,0:T(8,128)} async-done(((f32[8,64,64]{1,2,0:T(8,128)}), f32[8,64,64]{1,2,0:T(8,128)}) %all-reduce.4.cloned.1.call-update) | async-done | bytes 131088 | tf_op jit(solution)/shard_map/psum | solution.py:49
  443.3 46.9 %custom-call.7 = f32[8,64,64]{2,1,0:T(8,128)S(1)} custom-call(f32[8,64,64]{2,1,0:T(8,128)S(1)} %fusion.11), custom_call_target="Cholesky" | custom-call | tf_op jit(solution)/shard_map/jit(cholesky)/cholesky | solution.py:50
  490.5 39.3 %custom-call.8 = f32[8,1,64,64]{2,3,1,0:T(8,128)S(1)} custom-call(f32[8,1,64,64]{3,2,1,0:T(8,128)S(1)} %get-tuple-element.8), custom_call_target="InvertDiagBlocksLowerTriangular" | custom-call | tf_op jit(solution)/shard_map/triangular_solve | solution.py:52
  (32 shorter events, 25.0 us)
Async XLA Ops:
  7.2 97.4 %all-reduce.6.cloned.1.call-start = ((), (), s32[]{:S(2)}) async-start(), calls=%async_computation.2 | async-start | bytes 8388608
  23.9 0.7 copy-start
  167.7 25.2 %all-to-all-start = ((f32[32,1,2,8,1,256]{5,3,2,4,1,0:T(8,128)}), f32[32,1,2,8,1,256]{5,3,2,4,1,0:T(8,128)S(1)}, u32[]{:S(2)}, u32[]{:S(2)}) async-start(f32[32,1,2,8,1,256]{5,3,2,4,1,0:T(8,128)} %constant_dynamic-update-slice_fusion), calls=%async_computation | async-start | bytes 1048576 | tf_op jit(solution)/shard_map/all_to_all | solution.py:38
  177.8 263.4 %all-reduce.4.cloned.1.call-start = ((), (), s32[]{:S(2)}) async-start(), calls=%async_computation.1 | async-start | bytes 524288 | tf_op jit(solution)/shard_map/psum | solution.py:49
Sparse Core Ops, SparseCore 0:
  24.0 80.5 all-reduce.5
  194.6 246.5 all-reduce.3
